TPU v7x, 256 devices: a whole 4x4x8 slice. The times are simulated.
256 devices in a mesh: tm: 16 (over y, x), space: 16 (over z, core).
Axes of the slice: x: 4, y: 4, z: 8, core: 2. Of those that a mesh axis runs over, the one named last changes fastest.
Arguments:
- stored: bfloat16 [16, 288, 128, 128], P('tm', None, 'space'), may hold values from -6 to 6
- snapshot: int32 [16, 256], P('tm'), may hold values from 0 to 287, as said below
- balance_coef: float32 [128, 128], P('space'), may hold values from 0.5 to 2
- sea_mask: int32 [128, 128], P('space'), may hold values 0 or 1
Outputs:
- merged_basis: bfloat16 [256, 3, 128, 128], P('tm', None, 'space')
Inputs may be any that keep to these rules, and one draw needn't show every extreme that they name: `snapshot`: the 256 indices of one group are distinct.
All inputs are finite; a program needn't handle non-finite values. No bound on the sum of `sea_mask` on one device may be relied on, other than what follows from the above.
Results may differ from a plain program's by a relative error of at most 0.04.
Values may be sent and summed in bfloat16 or wider, within the bound.
No kernel may reach another device: no remote copies, remote signals or barrier semaphores. Data moves between devices by JAX's collectives and lax.ppermute only.
A program may use at most 64 MiB of HBM per device.

v0:
```python
import jax
import jax.numpy as jnp
from jax import lax
from jax.sharding import PartitionSpec as P

inv_root2 = 0.7071067811865476


def gathered_total(shard, axis):
    return lax.all_gather(shard, axis).astype(jnp.float32).sum(0)


def with_halo(cells, sides, width):
    for axis, dim in sides:
        count = lax.axis_size(axis)
        ends = count - 1
        head = lax.slice_in_dim(cells, 0, width, axis=dim)
        tail = lax.slice_in_dim(cells, cells.shape[dim] - width, cells.shape[dim], axis=dim)
        cells = jnp.concatenate(
            [
                lax.ppermute(tail, axis, [(i, (i + 1) % count) for i in range(ends)]),
                cells,
                lax.ppermute(head, axis, [((i + 1) % count, i) for i in range(ends)]),
            ],
            axis=dim,
        )
    return cells


def from_partner(shard, axis, stride):
    return lax.ppermute(shard, axis, [(i, i ^ 1 << stride) for i in range(lax.axis_size(axis))])


def balance(padded, balance_coef, sea_float):
    center = padded[:, 1:-1, :]
    values = center.astype(jnp.float32)
    east_cells = jnp.roll(values, -1, axis=2)
    west_cells = jnp.roll(values, 1, axis=2)
    zonal_flow = (-balance_coef * sea_float * (east_cells - west_cells)).astype(jnp.bfloat16)
    wide = padded.astype(jnp.float32)
    merid_flow = (balance_coef * sea_float * (wide[:, 2:, :] - wide[:, :-2, :])).astype(
        jnp.bfloat16
    )
    return jnp.stack([center, zonal_flow, merid_flow], axis=1).reshape(center.shape[0], -1)


def stack_pair(own_basis, other_basis, level_idx):
    own_bit = lax.axis_index("tm") // 2**level_idx % 2
    upper_part = jnp.where(own_bit == 0, own_basis, other_basis)
    lower_part = jnp.where(own_bit == 0, other_basis, own_basis)
    return jnp.concatenate([upper_part, lower_part], axis=0)


def merge_pair(own_basis, other_basis, level_idx, last_level):
    stacked = stack_pair(own_basis, other_basis, level_idx)
    members = own_basis.shape[0]
    local_gram = jnp.dot(stacked, stacked.T, preferred_element_type=jnp.float32)
    local_mixed = (local_gram[:, :members] + local_gram[:, members:]) * inv_root2
    mixed_cols = lax.psum(local_mixed, "space")
    normal = jnp.dot(
        mixed_cols.T,
        mixed_cols,
        precision=lax.Precision.HIGHEST,
        preferred_element_type=jnp.float32,
    )
    factor_low = jnp.linalg.cholesky(normal)
    rotation = (
        jax.scipy.linalg.solve_triangular(factor_low, mixed_cols.T, lower=True) * inv_root2
    ).astype(jnp.bfloat16)
    if last_level:
        member_share = rotation.shape[0] // lax.axis_size("tm")
        rotation = lax.dynamic_slice_in_dim(
            rotation, lax.axis_index("tm") * member_share, member_share, 0
        )
    return jnp.dot(rotation, stacked, preferred_element_type=jnp.float32).astype(jnp.bfloat16)


def body(stored, snapshot, balance_coef, sea_mask):
    sea_float = sea_mask.astype(jnp.float32)
    mean_state = jnp.mean(stored[0].astype(jnp.float32), axis=0)
    picked = jnp.take(stored[0], snapshot[0], axis=0)
    anomaly = ((picked.astype(jnp.float32) - mean_state) * sea_float).astype(jnp.bfloat16)
    padded = with_halo(anomaly, (("space", 1),), 1)
    basis_now = balance(padded, balance_coef, sea_float)
    levels = lax.axis_size("tm").bit_length() - 1
    first_level = 0
    other_padded = from_partner(padded, "tm", 0)
    partner = balance(other_padded, balance_coef, sea_float)
    basis_now = merge_pair(basis_now, partner, 0, levels == 1)
    first_level = 1
    for level_idx in range(first_level, levels):
        partner = from_partner(basis_now, "tm", level_idx)
        basis_now = merge_pair(basis_now, partner, level_idx, level_idx == levels - 1)
    return basis_now.reshape(basis_now.shape[0], 3, stored.shape[2], stored.shape[3])


def solution(mesh):
    placed = (P("tm", None, "space", None), P("tm", None), P("space", None), P("space", None))
    return jax.shard_map(
        body, mesh=mesh, in_specs=placed, out_specs=P("tm", None, "space", None), check_vma=False
    )
```

profile of v0, /device:TPU:1, one launch (start us, length us, event | category | flops | bytes accessed | tf_op | source)
XLA Modules:
  0.0 906.1 jit_solution(1723753065468144391)
XLA Ops:
  12.4 5.1 collective-permute-start.1
  33.1 7.0 collective-permute-done.2
  40.1 2.9 fusion.98
  54.2 3.0 fusion.10
  61.3 3.8 fusion.3
  66.2 112.5 %all-reduce.6.cloned.1.call-done = f32[512,256]{1,0:T(8,128)} async-done(((f32[512,256]{1,0:T(8,128)}), f32[512,256]{1,0:T(8,128)}) %all-reduce.6.cloned.1.call-update) | async-done | bytes 524304 | tf_op jit(solution)/shard_map/psum | solution.py:59
  181.2 11.7 %cholesky.214 = f32[128,128]{1,0:T(8,128)S(1)} custom-call(f32[128,128]{1,0:T(8,128)S(1)} %cholesky.346), custom_call_target="Cholesky" | custom-call | tf_op jit(solution)/shard_map/jit(cholesky)/cholesky | solution.py:66
  192.9 9.8 %custom-call.17 = f32[1,128,128]{1,2,0:T(8,128)S(1)} custom-call(f32[1,128,128]{2,1,0:T(8,128)S(1)} %get-tuple-element.118), custom_call_target="InvertDiagBlocksLowerTriangular" | custom-call | tf_op jit(solution)/shard_map/jit(cholesky)/cholesky | solution.py:66
  203.2 11.7 %cholesky.231 = f32[128,128]{1,0:T(8,128)S(1)} custom-call(f32[128,128]{1,0:T(8,128)S(1)} %convolution_subtract_fusion.7), custom_call_target="Cholesky" | custom-call | tf_op jit(solution)/shard_map/jit(cholesky)/cholesky | solution.py:66
  217.7 4.2 while.8
  221.8 19.7 %custom-call.18 = f32[2,128,128]{1,2,0:T(8,128)S(1)} custom-call(f32[2,128,128]{2,1,0:T(8,128)S(1)} %get-tuple-element.33), custom_call_target="InvertDiagBlocksLowerTriangular" | custom-call | tf_op jit(solution)/shard_map/jit(_solve_triangular)/triangular_solve | solution.py:68
  246.8 34.2 %collective-permute-done.3 = bf16[256,3072]{1,0:T(8,128)(2,1)} collective-permute-done((bf16[256,3072]{1,0:T(8,128)(2,1)S(1)}, bf16[256,3072]{1,0:T(8,128)(2,1)}, u32[]{:S(2)}, u32[]{:S(2)}) %collective-permute-start.3) | collective-permute-done | bytes 1572896 | tf_op jit(solution)/shard_map/ppermute | solution.py:31
  286.3 110.5 %all-reduce.8.cloned.1.call-done = f32[512,256]{1,0:T(8,128)} async-done(((f32[512,256]{1,0:T(8,128)}), f32[512,256]{1,0:T(8,128)}) %all-reduce.8.cloned.1.call-update) | async-done | bytes 524304 | tf_op jit(solution)/shard_map/psum | solution.py:59
  399.2 11.7 %cholesky.248 = f32[128,128]{1,0:T(8,128)S(1)} custom-call(f32[128,128]{1,0:T(8,128)S(1)} %cholesky.349), custom_call_target="Cholesky" | custom-call | tf_op jit(solution)/shard_map/jit(cholesky)/cholesky | solution.py:66
  411.0 9.8 %custom-call.19 = f32[1,128,128]{1,2,0:T(8,128)S(1)} custom-call(f32[1,128,128]{2,1,0:T(8,128)S(1)} %get-tuple-element.114), custom_call_target="InvertDiagBlocksLowerTriangular" | custom-call | tf_op jit(solution)/shard_map/jit(cholesky)/cholesky | solution.py:66
  421.3 11.7 %cholesky.265 = f32[128,128]{1,0:T(8,128)S(1)} custom-call(f32[128,128]{1,0:T(8,128)S(1)} %convolution_subtract_fusion.6), custom_call_target="Cholesky" | custom-call | tf_op jit(solution)/shard_map/jit(cholesky)/cholesky | solution.py:66
  435.7 4.1 while.9
  439.8 19.7 %custom-call.20 = f32[2,128,128]{1,2,0:T(8,128)S(1)} custom-call(f32[2,128,128]{2,1,0:T(8,128)S(1)} %get-tuple-element.34), custom_call_target="InvertDiagBlocksLowerTriangular" | custom-call | tf_op jit(solution)/shard_map/jit(_solve_triangular)/triangular_solve | solution.py:68
  464.3 34.4 %collective-permute-done.4 = bf16[256,3072]{1,0:T(8,128)(2,1)} collective-permute-done((bf16[256,3072]{1,0:T(8,128)(2,1)}, bf16[256,3072]{1,0:T(8,128)(2,1)}, u32[]{:S(2)}, u32[]{:S(2)}) %collective-permute-start.4) | collective-permute-done | bytes 1572896 | tf_op jit(solution)/shard_map/ppermute | solution.py:31
  503.8 110.7 %all-reduce.10.cloned.1.call-done = f32[512,256]{1,0:T(8,128)} async-done(((f32[512,256]{1,0:T(8,128)}), f32[512,256]{1,0:T(8,128)}) %all-reduce.10.cloned.1.call-update) | async-done | bytes 524304 | tf_op jit(solution)/shard_map/psum | solution.py:59
  617.0 11.7 %cholesky.282 = f32[128,128]{1,0:T(8,128)S(1)} custom-call(f32[128,128]{1,0:T(8,128)S(1)} %cholesky.352), custom_call_target="Cholesky" | custom-call | tf_op jit(solution)/shard_map/jit(cholesky)/cholesky | solution.py:66
  628.7 9.8 %custom-call.21 = f32[1,128,128]{1,2,0:T(8,128)S(1)} custom-call(f32[1,128,128]{2,1,0:T(8,128)S(1)} %get-tuple-element.110), custom_call_target="InvertDiagBlocksLowerTriangular" | custom-call | tf_op jit(solution)/shard_map/jit(cholesky)/cholesky | solution.py:66
  639.0 11.7 %cholesky.299 = f32[128,128]{1,0:T(8,128)S(1)} custom-call(f32[128,128]{1,0:T(8,128)S(1)} %convolution_subtract_fusion.5), custom_call_target="Cholesky" | custom-call | tf_op jit(solution)/shard_map/jit(cholesky)/cholesky | solution.py:66
  653.4 4.3 while.10
  657.8 19.7 %custom-call.22 = f32[2,128,128]{1,2,0:T(8,128)S(1)} custom-call(f32[2,128,128]{2,1,0:T(8,128)S(1)} %get-tuple-element.35), custom_call_target="InvertDiagBlocksLowerTriangular" | custom-call | tf_op jit(solution)/shard_map/jit(_solve_triangular)/triangular_solve | solution.py:68
  683.8 34.4 %collective-permute-done.5 = bf16[256,3072]{1,0:T(8,128)(2,1)} collective-permute-done((bf16[256,3072]{1,0:T(8,128)(2,1)}, bf16[256,3072]{1,0:T(8,128)(2,1)}, u32[]{:S(2)}, u32[]{:S(2)}) %collective-permute-start.5) | collective-permute-done | bytes 1572896 | tf_op jit(solution)/shard_map/ppermute | solution.py:31
  723.0 111.0 %all-reduce.12.cloned.1.call-done = f32[512,256]{1,0:T(8,128)} async-done(((f32[512,256]{1,0:T(8,128)}), f32[512,256]{1,0:T(8,128)}) %all-reduce.12.cloned.1.call-update) | async-done | bytes 524304 | tf_op jit(solution)/shard_map/psum | solution.py:59
  836.4 11.7 %cholesky.316 = f32[128,128]{1,0:T(8,128)S(1)} custom-call(f32[128,128]{1,0:T(8,128)S(1)} %cholesky.355), custom_call_target="Cholesky" | custom-call | tf_op jit(solution)/shard_map/jit(cholesky)/cholesky | solution.py:66
  848.2 9.8 %custom-call.23 = f32[1,128,128]{1,2,0:T(8,128)S(1)} custom-call(f32[1,128,128]{2,1,0:T(8,128)S(1)} %get-tuple-element.106), custom_call_target="InvertDiagBlocksLowerTriangular" | custom-call | tf_op jit(solution)/shard_map/jit(cholesky)/cholesky | solution.py:66
  858.5 11.9 %cholesky.333 = f32[128,128]{1,0:T(8,128)S(1)} custom-call(f32[128,128]{1,0:T(8,128)S(1)} %convolution_subtract_fusion.4), custom_call_target="Cholesky" | custom-call | tf_op jit(solution)/shard_map/jit(cholesky)/cholesky | solution.py:66
  873.0 3.9 while.11
  877.0 19.7 %custom-call.24 = f32[2,128,128]{1,2,0:T(8,128)S(1)} custom-call(f32[2,128,128]{2,1,0:T(8,128)S(1)} %get-tuple-element.36), custom_call_target="InvertDiagBlocksLowerTriangular" | custom-call | tf_op jit(solution)/shard_map/jit(_solve_triangular)/triangular_solve | solution.py:68
  (193 shorter events, 104.6 us)
Async XLA Ops:
  6.5 172.2 %all-reduce.6.cloned.1.call-start = ((), (), s32[]{:S(2)}) async-start(), calls=%async_computation | async-start | bytes 1048576 | tf_op jit(solution)/shard_map/psum | solution.py:59
  11.9 8.1 copy-start
  12.4 7.6 collective-permute-start.1
  17.5 3.9 collective-permute-start
  23.0 17.1 %collective-permute-start.2 = (bf16[256,10,128]{2,0,1:T(8,128)(2,1)}, bf16[256,10,128]{2,0,1:T(8,128)(2,1)}, u32[]{:S(2)}, u32[]{:S(2)}) collective-permute-start(bf16[256,10,128]{2,0,1:T(8,128)(2,1)} %copy.45), channel_id=1, source_target_pairs={{0,16},{16,0},{32,48},{48,32},{64,80},{80,64},{96,112},{112,96},{1... | collective-permute-start | bytes 1966088 | tf_op jit(solution)/shard_map/ppermute | solution.py:31
  27.1 4.3 copy-start.20
  27.1 4.3 copy-start.21
  50.9 2.4 copy-start.1
  50.9 2.4 copy-start.6
  50.9 2.6 copy-start.7
  50.9 2.9 copy-start.8
  50.9 3.3 copy-start.9
  54.2 3.0 copy-start.10
  59.5 1.9 copy-start.11
  66.0 330.8 %all-reduce.8.cloned.1.call-start = ((), (), s32[]{:S(2)}) async-start(), calls=%async_computation.1 | async-start | bytes 1048576 | tf_op jit(solution)/shard_map/psum | solution.py:59
  181.1 60.4 %copy-start.3 = (f32[512,256]{1,0:T(8,128)S(1)}, f32[512,256]{1,0:T(8,128)}, u32[]{:S(2)}) copy-start(f32[512,256]{1,0:T(8,128)} %all-reduce.6.cloned.1.call-done) | copy-start | bytes 1572868
  241.5 1.5 copy-start.12
  244.0 2.8 copy-start.19
  244.0 37.0 %collective-permute-start.3 = (bf16[256,3072]{1,0:T(8,128)(2,1)S(1)}, bf16[256,3072]{1,0:T(8,128)(2,1)}, u32[]{:S(2)}, u32[]{:S(2)}) collective-permute-start(bf16[256,3072]{1,0:T(8,128)(2,1)S(1)} %convolution_convert_fusion.2), channel_id=1, source_target_pairs={{0,32},{16,48},{32,0},{48,16},{64,96},{80,112},{96,64},{112,80},{1... | collective-permute-start | bytes 4718600 | tf_op jit(solution)/shard_map/ppermute | solution.py:31
  283.1 1.8 copy-start.15
  285.8 328.7 %all-reduce.10.cloned.1.call-start = ((), (), s32[]{:S(2)}) async-start(), calls=%async_computation.2 | async-start | bytes 1048576 | tf_op jit(solution)/shard_map/psum | solution.py:59
  399.2 60.3 %copy-start.4 = (f32[512,256]{1,0:T(8,128)S(1)}, f32[512,256]{1,0:T(8,128)}, u32[]{:S(2)}) copy-start(f32[512,256]{1,0:T(8,128)} %all-reduce.8.cloned.1.call-done) | copy-start | bytes 1572868
  459.5 1.5 copy-start.16
  463.1 35.6 %collective-permute-start.4 = (bf16[256,3072]{1,0:T(8,128)(2,1)}, bf16[256,3072]{1,0:T(8,128)(2,1)}, u32[]{:S(2)}, u32[]{:S(2)}) collective-permute-start(bf16[256,3072]{1,0:T(8,128)(2,1)} %convolution_convert_fusion.1), channel_id=1, source_target_pairs={{0,64},{16,80},{32,96},{48,112},{64,0},{80,16},{96,32},{112,48},{1... | collective-permute-start | bytes 4718600 | tf_op jit(solution)/shard_map/ppermute | solution.py:31
  500.8 1.8 copy-start.17
  503.6 330.4 %all-reduce.12.cloned.1.call-start = ((), (), s32[]{:S(2)}) async-start(), calls=%async_computation.3 | async-start | bytes 1048576 | tf_op jit(solution)/shard_map/psum | solution.py:59
  616.9 60.5 %copy-start.5 = (f32[512,256]{1,0:T(8,128)S(1)}, f32[512,256]{1,0:T(8,128)}, u32[]{:S(2)}) copy-start(f32[512,256]{1,0:T(8,128)} %all-reduce.10.cloned.1.call-done) | copy-start | bytes 1572868
  677.4 1.5 copy-start.18
  681.1 37.1 %collective-permute-start.5 = (bf16[256,3072]{1,0:T(8,128)(2,1)}, bf16[256,3072]{1,0:T(8,128)(2,1)}, u32[]{:S(2)}, u32[]{:S(2)}) collective-permute-start(bf16[256,3072]{1,0:T(8,128)(2,1)} %convolution_convert_fusion), channel_id=1, source_target_pairs={{0,128},{16,144},{32,160},{48,176},{64,192},{80,208},{96,224},{112... | collective-permute-start | bytes 4718600 | tf_op jit(solution)/shard_map/ppermute | solution.py:31
  720.3 1.8 copy-start.13
  836.4 60.3 %copy-start.2 = (f32[512,256]{1,0:T(8,128)S(1)}, f32[512,256]{1,0:T(8,128)}, u32[]{:S(2)}) copy-start(f32[512,256]{1,0:T(8,128)} %all-reduce.12.cloned.1.call-done) | copy-start | bytes 1572868
  896.7 1.5 copy-start.14
Sparse Core Ops, SparseCore 0:
  66.1 112.5 all-reduce.5
  286.0 110.8 all-reduce.7
  503.7 110.8 all-reduce.9
  723.1 110.8 all-reduce.11
where the time goes:
time: 914 us; the launch traced here: 906 us
  waiting for transfers between devices  557 us (61%)
  other arithmetic  241 us (26%)
  local copies, waits for them, and re-layouts  40.6 us (4%)
  matrix products  31.5 us (3%)
  between operations  19.1 us (2%)
  starting transfers between devices  15.7 us (2%)
    psum x4, waiting for transfers between devices, merge_pair(): mixed_cols = lax.psum(local_mixed, 'space')  445 us
    another operation x28, other arithmetic, merge_pair(): factor_low = jnp.linalg.cholesky(normal)  139 us
    ppermute x4, waiting for transfers between devices, from_partner(): lax.ppermute(shard, axis, [(i, i ^ 1 << stride) for i in range(lax.axis_s...  110 us
    another operation x9, other arithmetic, merge_pair(): jax.scipy.linalg.solve_triangular(factor_low, mixed_cols.T, lower=True)  78.8 us
  transfers between devices with their start and end apart: 10, of which 10 were waited for; matrix products, arithmetic and copies ran while one was open for 1% of the time, Pallas kernels for 0%

commit v1 on v0

--- a/solution.py
+++ b/solution.py
@@ -1,9 +1,17 @@
+import functools
 import jax
 import jax.numpy as jnp
 from jax import lax
 from jax.sharding import PartitionSpec as P
 
 inv_root2 = 0.7071067811865476
+
+
+def read_the_inputs(buf, peer_axis):
+    return jnp.sum(jax.lax.all_gather(buf, peer_axis), 0)
+
+
+convert_chunk_in = functools.partial(read_the_inputs, peer_axis="space")
 
 
 def gathered_total(shard, axis):
@@ -56,7 +64,7 @@
     members = own_basis.shape[0]
     local_gram = jnp.dot(stacked, stacked.T, preferred_element_type=jnp.float32)
     local_mixed = (local_gram[:, :members] + local_gram[:, members:]) * inv_root2
-    mixed_cols = lax.psum(local_mixed, "space")
+    mixed_cols = convert_chunk_in(local_mixed)
     normal = jnp.dot(
         mixed_cols.T,
         mixed_cols,

time: 914 us -> 706 us (0.77)
  waiting for transfers between devices: 557 us -> 337 us
  other arithmetic: 241 us -> 258 us
    psum x4 -> x0, waiting for transfers between devices: 445 us -> none  [merge_pair(): mixed_cols = lax.psum(local_mixed, 'space')]
    all_gather x0 -> x4, waiting for transfers between devices: none -> 224 us  [read_the_inputs(): return jnp.sum(jax.lax.all_gather(buf, peer_axis), 0)]
    reduce_sum x0 -> x4, other arithmetic: none -> 15.9 us  [read_the_inputs(): return jnp.sum(jax.lax.all_gather(buf, peer_axis), 0)]
where the time goes in v1:
time: 706 us; the launch traced here: 698 us
  waiting for transfers between devices  337 us (48%)
  other arithmetic  258 us (37%)
  local copies, waits for them, and re-layouts  42.1 us (6%)
  matrix products  25.8 us (4%)
  between operations  19.3 us (3%)
  starting transfers between devices  15.5 us (2%)
    all_gather x4, waiting for transfers between devices, read_the_inputs(): return jnp.sum(jax.lax.all_gather(buf, peer_axis), 0)  224 us
    another operation x28, other arithmetic, merge_pair(): factor_low = jnp.linalg.cholesky(normal)  139 us
    ppermute x4, waiting for transfers between devices, from_partner(): lax.ppermute(shard, axis, [(i, i ^ 1 << stride) for i in range(lax.axis_s...  111 us
    another operation x9, other arithmetic, merge_pair(): jax.scipy.linalg.solve_triangular(factor_low, mixed_cols.T, lower=True)  79.4 us
    reduce_sum x4, other arithmetic, read_the_inputs(): return jnp.sum(jax.lax.all_gather(buf, peer_axis), 0)  15.9 us
    another operation x29, local copies, waits for them, and re-layouts, merge_pair(): jax.scipy.linalg.solve_triangular(factor_low, mixed_cols.T, lower=True)  15.8 us
  transfers between devices with their start and end apart: 10, of which 10 were waited for; matrix products, arithmetic and copies ran while one was open for 1% of the time, Pallas kernels for 0%

profile of v1, /device:TPU:1, one launch (start us, length us, event | category | flops | bytes accessed | tf_op | source)
XLA Modules:
  0.0 697.9 jit_solution(8173415146015990328)
XLA Ops:
  12.4 5.1 collective-permute-start.1
  33.1 7.0 %collective-permute-done.2 = bf16[256,10,128]{2,0,1:T(8,128)(2,1)} collective-permute-done((bf16[256,10,128]{2,0,1:T(8,128)(2,1)}, bf16[256,10,128]{2,0,1:T(8,128)(2,1)}, u32[]{:S(2)}, u32[]{:S(2)}) %collective-permute-start.2) | collective-permute-done | bytes 655392 | tf_op jit(solution)/shard_map/ppermute | solution.py:39
  66.2 58.2 %all-gather.9.cloned.1.call-done = f32[8192,256]{1,0:T(8,128)} async-done(((f32[512,256]{1,0:T(8,128)}), f32[8192,256]{1,0:T(8,128)}) %all-gather.9.cloned.1.call-update) | async-done | bytes 8388624 | tf_op jit(solution)/shard_map/all_gather | solution.py:11
  124.4 4.0 reduce_sum.46
  129.8 11.7 %cholesky.214 = f32[128,128]{1,0:T(8,128)S(1)} custom-call(f32[128,128]{1,0:T(8,128)S(1)} %cholesky.346), custom_call_target="Cholesky" | custom-call | tf_op jit(solution)/shard_map/jit(cholesky)/cholesky | solution.py:74
  141.6 9.8 %custom-call.17 = f32[1,128,128]{1,2,0:T(8,128)S(1)} custom-call(f32[1,128,128]{2,1,0:T(8,128)S(1)} %get-tuple-element.118), custom_call_target="InvertDiagBlocksLowerTriangular" | custom-call | tf_op jit(solution)/shard_map/jit(cholesky)/cholesky | solution.py:74
  151.9 11.7 %cholesky.231 = f32[128,128]{1,0:T(8,128)S(1)} custom-call(f32[128,128]{1,0:T(8,128)S(1)} %convolution_subtract_fusion.7), custom_call_target="Cholesky" | custom-call | tf_op jit(solution)/shard_map/jit(cholesky)/cholesky | solution.py:74
  166.6 3.9 while.8
  170.5 19.7 %custom-call.18 = f32[2,128,128]{1,2,0:T(8,128)S(1)} custom-call(f32[2,128,128]{2,1,0:T(8,128)S(1)} %get-tuple-element.33), custom_call_target="InvertDiagBlocksLowerTriangular" | custom-call | tf_op jit(solution)/shard_map/jit(_solve_triangular)/triangular_solve | solution.py:76
  195.4 34.6 %collective-permute-done.3 = bf16[256,3072]{1,0:T(8,128)(2,1)} collective-permute-done((bf16[256,3072]{1,0:T(8,128)(2,1)S(1)}, bf16[256,3072]{1,0:T(8,128)(2,1)}, u32[]{:S(2)}, u32[]{:S(2)}) %collective-permute-start.3) | collective-permute-done | bytes 1572896 | tf_op jit(solution)/shard_map/ppermute | solution.py:39
  235.3 54.9 %all-gather.11.cloned.1.call-done = f32[8192,256]{1,0:T(8,128)} async-done(((f32[512,256]{1,0:T(8,128)}), f32[8192,256]{1,0:T(8,128)}) %all-gather.11.cloned.1.call-update) | async-done | bytes 8388624 | tf_op jit(solution)/shard_map/all_gather | solution.py:11
  290.2 4.0 reduce_sum.47
  295.6 11.7 %cholesky.248 = f32[128,128]{1,0:T(8,128)S(1)} custom-call(f32[128,128]{1,0:T(8,128)S(1)} %cholesky.349), custom_call_target="Cholesky" | custom-call | tf_op jit(solution)/shard_map/jit(cholesky)/cholesky | solution.py:74
  307.4 9.8 %custom-call.19 = f32[1,128,128]{1,2,0:T(8,128)S(1)} custom-call(f32[1,128,128]{2,1,0:T(8,128)S(1)} %get-tuple-element.114), custom_call_target="InvertDiagBlocksLowerTriangular" | custom-call | tf_op jit(solution)/shard_map/jit(cholesky)/cholesky | solution.py:74
  317.7 11.7 %cholesky.265 = f32[128,128]{1,0:T(8,128)S(1)} custom-call(f32[128,128]{1,0:T(8,128)S(1)} %convolution_subtract_fusion.6), custom_call_target="Cholesky" | custom-call | tf_op jit(solution)/shard_map/jit(cholesky)/cholesky | solution.py:74
  336.2 19.7 %custom-call.20 = f32[2,128,128]{1,2,0:T(8,128)S(1)} custom-call(f32[2,128,128]{2,1,0:T(8,128)S(1)} %get-tuple-element.34), custom_call_target="InvertDiagBlocksLowerTriangular" | custom-call | tf_op jit(solution)/shard_map/jit(_solve_triangular)/triangular_solve | solution.py:76
  360.7 34.8 %collective-permute-done.4 = bf16[256,3072]{1,0:T(8,128)(2,1)} collective-permute-done((bf16[256,3072]{1,0:T(8,128)(2,1)}, bf16[256,3072]{1,0:T(8,128)(2,1)}, u32[]{:S(2)}, u32[]{:S(2)}) %collective-permute-start.4) | collective-permute-done | bytes 1572896 | tf_op jit(solution)/shard_map/ppermute | solution.py:39
  400.3 55.4 %all-gather.13.cloned.1.call-done = f32[8192,256]{1,0:T(8,128)} async-done(((f32[512,256]{1,0:T(8,128)}), f32[8192,256]{1,0:T(8,128)}) %all-gather.13.cloned.1.call-update) | async-done | bytes 8388624 | tf_op jit(solution)/shard_map/all_gather | solution.py:11
  455.7 4.0 reduce_sum.48
  461.1 11.7 %cholesky.282 = f32[128,128]{1,0:T(8,128)S(1)} custom-call(f32[128,128]{1,0:T(8,128)S(1)} %cholesky.352), custom_call_target="Cholesky" | custom-call | tf_op jit(solution)/shard_map/jit(cholesky)/cholesky | solution.py:74
  472.9 9.8 %custom-call.21 = f32[1,128,128]{1,2,0:T(8,128)S(1)} custom-call(f32[1,128,128]{2,1,0:T(8,128)S(1)} %get-tuple-element.110), custom_call_target="InvertDiagBlocksLowerTriangular" | custom-call | tf_op jit(solution)/shard_map/jit(cholesky)/cholesky | solution.py:74
  483.1 11.7 %cholesky.299 = f32[128,128]{1,0:T(8,128)S(1)} custom-call(f32[128,128]{1,0:T(8,128)S(1)} %convolution_subtract_fusion.5), custom_call_target="Cholesky" | custom-call | tf_op jit(solution)/shard_map/jit(cholesky)/cholesky | solution.py:74
  497.9 3.9 while.10
  501.9 19.7 %custom-call.22 = f32[2,128,128]{1,2,0:T(8,128)S(1)} custom-call(f32[2,128,128]{2,1,0:T(8,128)S(1)} %get-tuple-element.35), custom_call_target="InvertDiagBlocksLowerTriangular" | custom-call | tf_op jit(solution)/shard_map/jit(_solve_triangular)/triangular_solve | solution.py:76
  527.8 34.8 %collective-permute-done.5 = bf16[256,3072]{1,0:T(8,128)(2,1)} collective-permute-done((bf16[256,3072]{1,0:T(8,128)(2,1)}, bf16[256,3072]{1,0:T(8,128)(2,1)}, u32[]{:S(2)}, u32[]{:S(2)}) %collective-permute-start.5) | collective-permute-done | bytes 1572896 | tf_op jit(solution)/shard_map/ppermute | solution.py:39
  567.4 55.4 %all-gather.15.cloned.1.call-done = f32[8192,256]{1,0:T(8,128)} async-done(((f32[512,256]{1,0:T(8,128)}), f32[8192,256]{1,0:T(8,128)}) %all-gather.15.cloned.1.call-update) | async-done | bytes 8388624 | tf_op jit(solution)/shard_map/all_gather | solution.py:11
  622.8 4.0 reduce_sum.49
  628.2 11.7 %cholesky.316 = f32[128,128]{1,0:T(8,128)S(1)} custom-call(f32[128,128]{1,0:T(8,128)S(1)} %cholesky.355), custom_call_target="Cholesky" | custom-call | tf_op jit(solution)/shard_map/jit(cholesky)/cholesky | solution.py:74
  640.0 9.8 %custom-call.23 = f32[1,128,128]{1,2,0:T(8,128)S(1)} custom-call(f32[1,128,128]{2,1,0:T(8,128)S(1)} %get-tuple-element.106), custom_call_target="InvertDiagBlocksLowerTriangular" | custom-call | tf_op jit(solution)/shard_map/jit(cholesky)/cholesky | solution.py:74
  650.3 11.9 %cholesky.333 = f32[128,128]{1,0:T(8,128)S(1)} custom-call(f32[128,128]{1,0:T(8,128)S(1)} %convolution_subtract_fusion.4), custom_call_target="Cholesky" | custom-call | tf_op jit(solution)/shard_map/jit(cholesky)/cholesky | solution.py:74
  664.9 4.0 while.11
  668.9 19.7 %custom-call.24 = f32[2,128,128]{1,2,0:T(8,128)S(1)} custom-call(f32[2,128,128]{2,1,0:T(8,128)S(1)} %get-tuple-element.36), custom_call_target="InvertDiagBlocksLowerTriangular" | custom-call | tf_op jit(solution)/shard_map/jit(_solve_triangular)/triangular_solve | solution.py:76
  (193 shorter events, 114.5 us)
Async XLA Ops:
  6.5 117.9 %all-gather.9.cloned.1.call-start = ((), (), s32[]{:S(2)}) async-start(), calls=%async_computation | async-start | bytes 8912896 | tf_op jit(solution)/shard_map/all_gather | solution.py:11
  11.9 8.1 %copy-start = (bf16[256,8,128]{2,1,0:T(8,128)(2,1)}, bf16[256,8,128]{2,1,0:T(8,128)(2,1)S(1)}, u32[]{:S(2)}) copy-start(bf16[256,8,128]{2,1,0:T(8,128)(2,1)S(1)} %gather_fusion) | copy-start | bytes 1572868
  12.4 7.6 %collective-permute-start.1 = (bf16[256,1,128]{2,1,0:T(2,128)(2,1)S(1)}, bf16[256,1,128]{2,1,0:T(2,128)(2,1)S(1)}, u32[]{:S(2)}, u32[]{:S(2)}) collective-permute-start(bf16[256,1,128]{2,1,0:T(2,128)(2,1)S(1)} %get-tuple-element.102), channel_id=1, source_target_pairs={{1,0},{2,1},{3,2},{4,3},{5,4},{6,5},{7,6},{8,7},{9,8},{10,9},{11,1... | collective-permute-start | bytes 196616 | tf_op jit(solution)/shard_map/ppermute | solution.py:31
  17.5 3.9 collective-permute-start
  23.0 17.1 %collective-permute-start.2 = (bf16[256,10,128]{2,0,1:T(8,128)(2,1)}, bf16[256,10,128]{2,0,1:T(8,128)(2,1)}, u32[]{:S(2)}, u32[]{:S(2)}) collective-permute-start(bf16[256,10,128]{2,0,1:T(8,128)(2,1)} %copy.41), channel_id=1, source_target_pairs={{0,16},{16,0},{32,48},{48,32},{64,80},{80,64},{96,112},{112,96},{1... | collective-permute-start | bytes 1966088 | tf_op jit(solution)/shard_map/ppermute | solution.py:39
  27.1 4.3 copy-start.16
  27.1 4.3 copy-start.17
  50.8 2.4 copy-start.1
  50.9 2.4 copy-start.2
  50.9 2.6 copy-start.3
  50.9 2.9 copy-start.4
  50.9 3.3 copy-start.5
  54.1 3.0 copy-start.6
  59.5 1.9 copy-start.7
  66.0 224.3 %all-gather.11.cloned.1.call-start = ((), (), s32[]{:S(2)}) async-start(), calls=%async_computation.1 | async-start | bytes 8912896 | tf_op jit(solution)/shard_map/all_gather | solution.py:11
  190.2 1.4 copy-start.8
  192.6 2.8 copy-start.15
  192.6 37.4 %collective-permute-start.3 = (bf16[256,3072]{1,0:T(8,128)(2,1)S(1)}, bf16[256,3072]{1,0:T(8,128)(2,1)}, u32[]{:S(2)}, u32[]{:S(2)}) collective-permute-start(bf16[256,3072]{1,0:T(8,128)(2,1)S(1)} %convolution_convert_fusion.2), channel_id=1, source_target_pairs={{0,32},{16,48},{32,0},{48,16},{64,96},{80,112},{96,64},{112,80},{1... | collective-permute-start | bytes 4718600 | tf_op jit(solution)/shard_map/ppermute | solution.py:39
  232.1 1.8 copy-start.11
  234.8 220.8 %all-gather.13.cloned.1.call-start = ((), (), s32[]{:S(2)}) async-start(), calls=%async_computation.2 | async-start | bytes 8912896 | tf_op jit(solution)/shard_map/all_gather | solution.py:11
  355.9 1.4 copy-start.12
  359.5 36.0 %collective-permute-start.4 = (bf16[256,3072]{1,0:T(8,128)(2,1)}, bf16[256,3072]{1,0:T(8,128)(2,1)}, u32[]{:S(2)}, u32[]{:S(2)}) collective-permute-start(bf16[256,3072]{1,0:T(8,128)(2,1)} %convolution_convert_fusion.1), channel_id=1, source_target_pairs={{0,64},{16,80},{32,96},{48,112},{64,0},{80,16},{96,32},{112,48},{1... | collective-permute-start | bytes 4718600 | tf_op jit(solution)/shard_map/ppermute | solution.py:39
  397.5 1.8 copy-start.13
  400.3 222.6 %all-gather.15.cloned.1.call-start = ((), (), s32[]{:S(2)}) async-start(), calls=%async_computation.3 | async-start | bytes 8912896 | tf_op jit(solution)/shard_map/all_gather | solution.py:11
  521.6 1.4 copy-start.14
  525.1 37.5 %collective-permute-start.5 = (bf16[256,3072]{1,0:T(8,128)(2,1)}, bf16[256,3072]{1,0:T(8,128)(2,1)}, u32[]{:S(2)}, u32[]{:S(2)}) collective-permute-start(bf16[256,3072]{1,0:T(8,128)(2,1)} %convolution_convert_fusion), channel_id=1, source_target_pairs={{0,128},{16,144},{32,160},{48,176},{64,192},{80,208},{96,224},{112... | collective-permute-start | bytes 4718600 | tf_op jit(solution)/shard_map/ppermute | solution.py:39
  564.7 1.8 copy-start.9
  688.6 1.4 copy-start.10
Sparse Core Ops, SparseCore 0:
  66.1 58.2 all-gather.8
  234.9 55.2 all-gather.10
  400.4 55.2 all-gather.12
  567.6 55.2 all-gather.14
